TPU v7x, 32 devices: a whole 2x2x4 slice. The times are simulated.
32 devices in a mesh: src: 4 (over x, core), ep: 8 (over z, y).
Axes of the slice: x: 2, y: 2, z: 4, core: 2. Of those that a mesh axis runs over, the one named last changes fastest.
Arguments:
- log_conductivity: float32 [8, 16, 32, 128], P('ep'), may hold values from -3 to 3
- forward_field: float32 [8, 4, 16, 32, 128], P('ep', 'src'), may hold values from -6 to 6
- adjoint_field: float32 [8, 4, 16, 32, 128], P('ep', 'src'), may hold values from -6 to 6
- source_cells: int32 [4, 2], P('src'), may hold values from 0 to 65535
- receiver_cells: int32 [128], replicated, may hold values from 0 to 65535
- observed: float32 [8, 4, 128], P('ep', 'src'), may hold values from -6 to 6
- split_term: float32 [6, 65536], P(None, ('src', 'ep')), may hold values from -1.2 to 1.2
- dual_term: float32 [6, 65536], P(None, ('src', 'ep')), may hold values from -1.2 to 1.2
Outputs:
- model_out: float32 [8, 16, 32, 128], P('ep')
- split_out: float32 [6, 65536], P(None, ('src', 'ep'))
- dual_out: float32 [6, 65536], P(None, ('src', 'ep'))
Inputs may be any that keep to these rules, and one draw needn't show every extreme that they name: `source_cells`: source and receiver cells may repeat; a source's two electrodes may coincide.
All inputs are finite; a program needn't handle non-finite values.
Results may differ from a plain program's by a relative error of at most 0.0003.
Values sent between devices are 32-bit elements; how exact they have to be, the bound alone decides.
No kernel may reach another device: no remote copies, remote signals or barrier semaphores. Data moves between devices by JAX's collectives and lax.ppermute only.
A program may use at most 128 MiB of HBM per device.

v0:
```python
import jax
import jax.numpy as jnp
from jax import lax
from jax.sharding import PartitionSpec as P

SWEEPS = 4
MASS_TERM = 0.5
RELAXATION = 0.8
CURRENT = 4.0
DATA_WEIGHT = 8.0
STEP_SIZE = 0.5
PENALTY = 64.0
THRESHOLD = 0.1


def pad_side(values, dim_index, at_low):
    widths = [(0, 0)] * values.ndim
    widths[dim_index] = (0, 1) if at_low else (1, 0)
    return jnp.pad(values, widths)


def conductances(conductivity):
    face_weights = []
    diagonal = MASS_TERM * conductivity
    ndims = conductivity.ndim
    for dim_index in range(ndims - 3, ndims):
        length = conductivity.shape[dim_index]
        lower_cells = lax.slice_in_dim(conductivity, 0, length - 1, axis=dim_index)
        upper_cells = lax.slice_in_dim(conductivity, 1, length, axis=dim_index)
        face_weight = 0.5 * (lower_cells + upper_cells)
        face_weights.append(face_weight)
        diagonal = (
            diagonal
            + pad_side(face_weight, dim_index, True)
            + pad_side(face_weight, dim_index, False)
        )
    return (face_weights, diagonal)


def operate(iterate, conductivity, face_weights):
    result = MASS_TERM * conductivity * iterate
    ndims = iterate.ndim
    for position, dim_index in enumerate(range(ndims - 3, ndims)):
        length = iterate.shape[dim_index]
        face_flux = face_weights[position] * (
            lax.slice_in_dim(iterate, 1, length, axis=dim_index)
            - lax.slice_in_dim(iterate, 0, length - 1, axis=dim_index)
        )
        result = (
            result - pad_side(face_flux, dim_index, True) + pad_side(face_flux, dim_index, False)
        )
    return result


def relax(iterate, right_side, conductivity, face_weights, diagonal):
    for sweep_index in range(SWEEPS):
        iterate = (
            iterate
            + RELAXATION * (right_side - operate(iterate, conductivity, face_weights)) / diagonal
        )
    return iterate


def source_field(source_cells, cell_count):
    source_count = source_cells.shape[0]
    row_index = jnp.arange(source_count, dtype=jnp.int32)[:, None] * jnp.ones((1, 2), jnp.int32)
    polarity = jnp.broadcast_to(jnp.array([CURRENT, -CURRENT], jnp.float32), (source_count, 2))
    return (
        jnp.zeros((source_count, cell_count), jnp.float32).at[row_index, source_cells].add(polarity)
    )


def sweep_epoch(model_log, forward, adjoint, sources, receiver_cells, observed):
    grid_shape = forward.shape
    conductivity = jnp.exp(model_log)[None]
    face_weights, diagonal = conductances(conductivity)
    forward = relax(forward, sources.reshape(grid_shape), conductivity, face_weights, diagonal)
    flat_field = forward.reshape(grid_shape[0], -1)
    misfit = flat_field[:, receiver_cells] - observed
    adjoint_source = (
        jnp.zeros_like(flat_field)
        .at[:, receiver_cells]
        .add(DATA_WEIGHT * misfit)
        .reshape(grid_shape)
    )
    adjoint = relax(adjoint, adjoint_source, conductivity, face_weights, diagonal)
    gradient = conductivity[0] * jnp.sum(forward * adjoint, axis=0)
    return (forward, adjoint, gradient)


def temporal_factor(epochs):
    second = (
        jnp.eye(epochs - 2, epochs, dtype=jnp.float32)
        - 2.0 * jnp.eye(epochs - 2, epochs, k=1, dtype=jnp.float32)
        + jnp.eye(epochs - 2, epochs, k=2, dtype=jnp.float32)
    )
    matrix = jnp.eye(epochs, dtype=jnp.float32) + PENALTY * jnp.dot(
        second.T, second, precision=lax.Precision.HIGHEST
    )
    return jnp.linalg.cholesky(matrix)


def difference(values):
    return values[:-2] - 2.0 * values[1:-1] + values[2:]


def difference_adjoint(values):
    widths_low = [(0, 2), (0, 0)]
    widths_mid = [(1, 1), (0, 0)]
    widths_high = [(2, 0), (0, 0)]
    return (
        jnp.pad(values, widths_low)
        - 2.0 * jnp.pad(values, widths_mid)
        + jnp.pad(values, widths_high)
    )


def splitting_update(local_rhs, split_term, dual_term, factor):
    right_side = local_rhs + PENALTY * difference_adjoint(split_term - dual_term)
    updated = jax.scipy.linalg.cho_solve((factor, True), right_side)
    shifted = difference(updated) + dual_term
    split_term = shifted - jnp.clip(shifted, -THRESHOLD, THRESHOLD)
    dual_term = shifted - split_term
    return (updated, split_term, dual_term)


def on_device(
    log_conductivity,
    forward_field,
    adjoint_field,
    source_cells,
    receiver_cells,
    observed,
    split_term,
    dual_term,
):
    slab_epochs, size_x, size_y, size_z = log_conductivity.shape
    cell_count = size_x * size_y * size_z
    share_cells = cell_count // lax.axis_size("src")
    offset = lax.axis_index("src") * share_cells
    total_epochs = slab_epochs * lax.axis_size("ep")
    sources = source_field(source_cells, cell_count)
    factor = temporal_factor(total_epochs)
    sweeper = jax.vmap(sweep_epoch, in_axes=(0, 0, 0, None, None, 0))
    model_log = log_conductivity
    forward = forward_field
    adjoint = adjoint_field
    forward, adjoint, partial_terms = sweeper(
        model_log, forward, adjoint, sources, receiver_cells, observed
    )
    partial_terms = partial_terms.reshape(slab_epochs, cell_count)
    summed = lax.psum(partial_terms, "src")
    gradient_share = lax.dynamic_slice_in_dim(summed, offset, share_cells, 1)
    model_share = lax.dynamic_slice_in_dim(
        model_log.reshape(slab_epochs, cell_count), offset, share_cells, 1
    )
    local_rhs = model_share - STEP_SIZE * gradient_share
    time_rhs = lax.all_to_all(local_rhs, "ep", split_axis=1, concat_axis=0, tiled=True)
    updated, split_term, dual_term = splitting_update(time_rhs, split_term, dual_term, factor)
    slab_share = lax.all_to_all(updated, "ep", split_axis=0, concat_axis=1, tiled=True)
    model_log = lax.all_gather(slab_share, "src", axis=1, tiled=True).reshape(
        slab_epochs, size_x, size_y, size_z
    )
    return (model_log, split_term, dual_term)


def solution(mesh):
    return jax.shard_map(
        on_device,
        mesh=mesh,
        in_specs=(
            P("ep", None, None, None),
            P("ep", "src", None, None, None),
            P("ep", "src", None, None, None),
            P("src", None),
            P(),
            P("ep", "src", None),
            P(None, ("src", "ep")),
            P(None, ("src", "ep")),
        ),
        out_specs=(P("ep", None, None, None), P(None, ("src", "ep")), P(None, ("src", "ep"))),
        check_vma=False,
    )
```

profile of v0, /device:TPU:0, one launch (start us, length us, event | category | flops | bytes accessed | tf_op | source)
XLA Modules:
  0.0 93.7 jit_solution(12895999680581403792)
XLA Ops:
  7.2 1.0 %exponential_bitcast_fusion = f32[1,1,16,32,128]{4,3,2,1,0:T(8,128)S(1)} fusion(f32[1,16,32,128]{3,2,1,0:T(8,128)} %param.9), kind=kLoop, calls=%fused_computation.45 | loop fusion | bytes 524288 | tf_op jit(solution)/shard_map/vmap()/broadcast_in_dim | solution.py:75
  8.3 0.2 subtract_multiply_fusion
  8.5 0.1 subtract_multiply_fusion.1
  8.6 0.9 copy-done.2
  9.5 0.1 subtract_multiply_fusion.2
  9.7 0.7 subtract_multiply_fusion.5
  10.4 0.1 copy.36
  10.5 0.1 pad_bitcast_fusion
  10.6 0.2 fusion.52
  10.8 0.8 scatter_custom_fusion
  11.6 1.4 %divide_add_fusion.6 = (f32[1,1,16,32,128]{4,3,2,1,0:T(8,128)S(1)}, f32[1,1,16,32,128]{4,3,2,1,0:T(8,128)S(1)}) fusion(f32[1,1,16,32,128]{4,3,2,1,0:T(8,128)S(1)} %copy-done.2, f32[1,1,16,32,128]{4,3,2,1,0:T(8,128)S(1)} %bitcast.67, f32[1,1,16,32,127]{4,3,2,1,0:T(8,128)S(1)} %subtract_multiply_fusion.2, ...), kind=kLoop, calls=%fused_computation.41 | loop fusion | flops 1179648 | bytes 2830336 | tf_op jit(solution)/shard_map/vmap()/add | solution.py:58
  13.2 0.1 fusion.10
  13.3 0.3 divide_add_fusion.5
  13.7 0.1 fusion.8
  13.8 0.3 divide_add_fusion.4
  14.2 0.1 fusion.6
  14.3 0.5 copy-done.6
  14.8 0.2 divide_add_fusion.3
  15.1 1.1 %gather_fusion = f32[128]{0:T(128)S(1)} fusion(f32[65536]{0:T(1024)S(1)} %bitcast.71, s32[1024]{0:T(1024)S(1)} %pad_clamp_fusion), kind=kCustom, calls=%fused_computation | custom fusion | bytes 1536 | tf_op jit(solution)/shard_map/vmap()/gather | solution.py:79
  16.3 1.3 %scatter_custom_fusion.1 = f32[65536]{0:T(1024)S(1)} fusion(s32[128]{0:T(128)S(1)} %compare_select_fusion, f32[128]{0:T(128)S(1)} %fusion.55, f32[]{:T(128)} %constant.82.clone.1), kind=kCustom, calls=%fused_computation.62 | custom fusion | flops 128 | bytes 262148 | tf_op jit(solution)/shard_map/vmap()/scatter-add | solution.py:83
  17.6 0.3 divide_add_fusion.2
  18.0 0.1 fusion.4
  18.1 0.3 divide_add_fusion.1
  18.5 0.1 fusion.2
  18.6 0.3 divide_add_fusion
  19.0 0.1 fusion
  19.1 1.0 %bitcast_multiply_fusion = f32[1,16,32,128]{3,2,1,0:T(8,128)} fusion(f32[1,1,16,32,128]{4,3,2,1,0:T(8,128)S(1)} %divide_add_fusion.3, f32[1,1,16,32,128]{4,3,2,1,0:T(8,128)S(1)} %divide_add_fusion, f32[1,1,16,32,128]{4,3,2,1,0:T(8,128)S(1)} %get-tuple-element.12, f32[1,1,16,32,128]{4,3,2,1,0:T(8,128)S(1)} %bitcast.66, f32[1,1,16,32,127]{4,3,2,1,0:T(8,128)S(1)} %fusion, ...), kind=kLoop, calls=%fused_computation.32 | loop fusion | flops 917504 | bytes 2332672 | tf_op jit(solution)/shard_map/vmap()/mul | solution.py:87
  20.1 0.3 convert_add_fusion
  20.4 0.1 copy.27
  20.5 0.7 cholesky.17
  21.2 0.1 copy.28
  21.2 0.2 select_reduce_fusion
  21.4 0.6 compare_reduce_fusion
  22.0 32.9 %all-reduce.60.cloned.1.call-done = f32[1,65536]{1,0:T(1,128)} async-done(((f32[1,65536]{1,0:T(1,128)}), f32[1,65536]{1,0:T(1,128)}) %all-reduce.60.cloned.1.call-update) | async-done | bytes 262160 | tf_op jit(solution)/shard_map/psum | solution.py:152
  54.9 1.6 %multiply_subtract_fusion = f32[1,16384]{1,0:T(1,128)} fusion(f32[1,65536]{1,0:T(1,128)} %all-reduce.60.cloned.1.call-done, s32[]{:T(128)S(6)} %select_n.16, f32[1,65536]{1,0:T(1,128)S(1)} %bitcast.62), kind=kLoop, calls=%fused_computation.81 | loop fusion | flops 32768 | bytes 196612 | tf_op jit(solution)/shard_map/sub | solution.py:157
  56.5 5.6 %all-to-all-start = ((f32[1,8,2048]{2,0,1:T(1,128)}), f32[1,8,2048]{2,0,1:T(1,128)S(1)}, u32[]{:S(2)}, u32[]{:S(2)}) async-start(f32[1,8,2048]{2,0,1:T(1,128)} %bitcast.14), calls=%async_computation | async-start | bytes 131072 | tf_op jit(solution)/shard_map/all_to_all | solution.py:158
  62.1 0.6 select_select_fusion
  62.8 0.1 copy.30
  62.9 0.6 custom-call.10
  63.5 5.5 %all-to-all-done = f32[1,8,2048]{2,0,1:T(1,128)S(1)} async-done(((f32[1,8,2048]{2,0,1:T(1,128)}), f32[1,8,2048]{2,0,1:T(1,128)S(1)}, u32[]{:S(2)}, u32[]{:S(2)}) %all-to-all-start) | async-done | bytes 65568 | tf_op jit(solution)/shard_map/all_to_all | solution.py:158
  69.0 0.3 fusion.27
  69.3 0.2 fusion.39
  69.5 0.7 copy.33
  70.2 3.4 %all-to-all-start.1 = ((f32[8,1,2048]{2,1,0:T(1,128)}), f32[8,1,2048]{2,1,0:T(1,128)S(1)}, u32[]{:S(2)}, u32[]{:S(2)}) async-start(f32[8,1,2048]{2,1,0:T(1,128)} %copy.33), calls=%async_computation.1 | async-start | bytes 131072 | tf_op jit(solution)/shard_map/all_to_all | solution.py:160
  73.6 0.7 fusion.61
  74.2 6.2 %all-to-all-done.1 = f32[8,1,2048]{2,1,0:T(1,128)S(1)} async-done(((f32[8,1,2048]{2,1,0:T(1,128)}), f32[8,1,2048]{2,1,0:T(1,128)S(1)}, u32[]{:S(2)}, u32[]{:S(2)}) %all-to-all-start.1) | async-done | bytes 65568 | tf_op jit(solution)/shard_map/all_to_all | solution.py:160
  80.4 5.8 %all_gather.3 = f32[1,65536]{1,0:T(1,128)S(1)} all-gather(f32[1,16384]{1,0:T(1,128)S(1)} %bitcast.75), channel_id=1, replica_groups=mesh['src'=4,'ep'=8] {'src'}, dimensions={1}, use_global_device_ids=true | all-gather | bytes 327680 | tf_op jit(solution)/shard_map/all_gather | solution.py:161
  86.2 0.7 copy.43
  (37 shorter events, 0.7 us)
Async XLA Ops:
  7.2 1.1 %copy-start.1 = (f32[1,1,16,32,128]{4,3,2,1,0:T(8,128)S(1)}, f32[1,1,16,32,128]{4,3,2,1,0:T(8,128)}, u32[]{:S(2)}) copy-start(f32[1,1,16,32,128]{4,3,2,1,0:T(8,128)} %param.11) | copy-start | bytes 786436
  7.2 47.8 %all-reduce.60.cloned.1.call-start = ((), (), s32[]{:S(2)}) async-start(), calls=%async_computation.2 | async-start | bytes 524288 | tf_op jit(solution)/shard_map/psum | solution.py:152
  8.6 1.0 %copy-start.2 = (f32[1,1,16,32,128]{4,3,2,1,0:T(8,128)S(1)}, f32[1,1,16,32,128]{4,3,2,1,0:T(8,128)}, u32[]{:S(2)}) copy-start(f32[1,1,16,32,128]{4,3,2,1,0:T(8,128)} %param.10) | copy-start | bytes 786436
  9.7 0.7 copy-start.5
  10.4 1.2 %copy-start = (f32[1,16,32,128]{3,2,1,0:T(8,128)S(1)}, f32[1,16,32,128]{3,2,1,0:T(8,128)}, u32[]{:S(2)}) copy-start(f32[1,16,32,128]{3,2,1,0:T(8,128)} %param.9) | copy-start | bytes 786436
  14.2 0.7 copy-start.6
  15.1 1.2 %copy-start.7 = (f32[1,1,128]{2,1,0:T(1,128)S(1)}, f32[1,1,128]{2,1,0:T(1,128)}, u32[]{:S(2)}) copy-start(f32[1,1,128]{2,1,0:T(1,128)} %param.14) | copy-start | bytes 1540
  56.5 7.0 %copy-start.3 = (f32[6,2048]{1,0:T(8,128)S(1)}, f32[6,2048]{1,0:T(8,128)}, u32[]{:S(2)}) copy-start(f32[6,2048]{1,0:T(8,128)} %param.16) | copy-start | bytes 147460
  56.5 7.0 %copy-start.4 = (f32[6,2048]{1,0:T(8,128)S(1)}, f32[6,2048]{1,0:T(8,128)}, u32[]{:S(2)}) copy-start(f32[6,2048]{1,0:T(8,128)} %param.15) | copy-start | bytes 147460
  56.5 12.6 %all-to-all-start = ((f32[1,8,2048]{2,0,1:T(1,128)}), f32[1,8,2048]{2,0,1:T(1,128)S(1)}, u32[]{:S(2)}, u32[]{:S(2)}) async-start(f32[1,8,2048]{2,0,1:T(1,128)} %bitcast.14), calls=%async_computation | async-start | bytes 131072 | tf_op jit(solution)/shard_map/all_to_all | solution.py:158
  70.2 10.2 %all-to-all-start.1 = ((f32[8,1,2048]{2,1,0:T(1,128)}), f32[8,1,2048]{2,1,0:T(1,128)S(1)}, u32[]{:S(2)}, u32[]{:S(2)}) async-start(f32[8,1,2048]{2,1,0:T(1,128)} %copy.33), calls=%async_computation.1 | async-start | bytes 131072 | tf_op jit(solution)/shard_map/all_to_all | solution.py:160
Sparse Core Ops, SparseCore 0:
  20.2 34.6 all-reduce.59
where the time goes:
time: 94.2 us; the launch traced here: 93.7 us
  waiting for transfers between devices  44.6 us (47%)
  between operations  14.4 us (15%)
  other arithmetic  13.8 us (15%)
  starting transfers between devices  9.04 us (10%)
  blocking collectives  5.77 us (6%)
  local copies, waits for them, and re-layouts  5.39 us (6%)
    psum x1, waiting for transfers between devices, on_device(): summed = lax.psum(partial_terms, 'src')  32.9 us
    all_to_all x1, waiting for transfers between devices, on_device(): lax.all_to_all(updated, 'ep', split_axis=0, concat_axis=1, tiled=True)  6.16 us
    all_gather x1, blocking collectives, on_device(): lax.all_gather(slab_share, 'src', axis=1, tiled=True)  5.77 us
    all_to_all x1, starting transfers between devices, on_device(): lax.all_to_all(local_rhs, 'ep', split_axis=1, concat_axis=0, tiled=True)  5.65 us
    all_to_all x1, waiting for transfers between devices, on_device(): lax.all_to_all(local_rhs, 'ep', split_axis=1, concat_axis=0, tiled=True)  5.53 us
    all_to_all x1, starting transfers between devices, on_device(): lax.all_to_all(updated, 'ep', split_axis=0, concat_axis=1, tiled=True)  3.35 us
    add x7, other arithmetic, relax(): iterate + RELAXATION * (right_side - operate(iterate, conductivity, face_...  2.93 us
    mul x24, other arithmetic, operate(): face_weights[position]  2.55 us
  transfers between devices with their start and end apart: 3, of which 3 were waited for; matrix products, arithmetic and copies ran while one was open for 4% of the time, Pallas kernels for 0%

commit v1 on v0

--- a/solution.py
+++ b/solution.py
@@ -149,7 +149,7 @@
         model_log, forward, adjoint, sources, receiver_cells, observed
     )
     partial_terms = partial_terms.reshape(slab_epochs, cell_count)
-    summed = lax.psum(partial_terms, "src")
+    summed = jnp.sum(lax.all_gather(partial_terms, "src"), axis=0)
     gradient_share = lax.dynamic_slice_in_dim(summed, offset, share_cells, 1)
     model_share = lax.dynamic_slice_in_dim(
         model_log.reshape(slab_epochs, cell_count), offset, share_cells, 1

time: 94.2 us -> 80.3 us (0.85)
  waiting for transfers between devices: 44.6 us -> 29.4 us
  other arithmetic: 13.8 us -> 15.2 us
    psum x1 -> x0, waiting for transfers between devices: 32.9 us -> none  [on_device(): summed = lax.psum(partial_terms, 'src')]
    all_gather x0 -> x1, waiting for transfers between devices: none -> 17.7 us  [on_device(): summed = jnp.sum(lax.all_gather(partial_terms, 'src'), axis=0)]
    reduce_sum x0 -> x1, other arithmetic: none -> 2.19 us  [on_device(): summed = jnp.sum(lax.all_gather(partial_terms, 'src'), axis=0)]
  transfers between devices with their start and end apart: 3 -> 3, of which waited for: 3 -> 3; matrix products, arithmetic and copies ran while one was open for 4% -> 5% of each run, Pallas kernels for 0% -> 0%
where the time goes in v1:
time: 80.3 us; the launch traced here: 79.9 us
  waiting for transfers between devices  29.4 us (37%)
  other arithmetic  15.2 us (19%)
  between operations  14.4 us (18%)
  starting transfers between devices  9.04 us (11%)
  blocking collectives  5.77 us (7%)
  local copies, waits for them, and re-layouts  5.39 us (7%)
    all_gather x1, waiting for transfers between devices, on_device(): summed = jnp.sum(lax.all_gather(partial_terms, 'src'), axis=0)  17.7 us
    all_to_all x1, waiting for transfers between devices, on_device(): lax.all_to_all(updated, 'ep', split_axis=0, concat_axis=1, tiled=True)  6.16 us
    all_gather x1, blocking collectives, on_device(): lax.all_gather(slab_share, 'src', axis=1, tiled=True)  5.77 us
    all_to_all x1, starting transfers between devices, on_device(): lax.all_to_all(local_rhs, 'ep', split_axis=1, concat_axis=0, tiled=True)  5.65 us
    all_to_all x1, waiting for transfers between devices, on_device(): lax.all_to_all(local_rhs, 'ep', split_axis=1, concat_axis=0, tiled=True)  5.53 us
    all_to_all x1, starting transfers between devices, on_device(): lax.all_to_all(updated, 'ep', split_axis=0, concat_axis=1, tiled=True)  3.35 us
    add x7, other arithmetic, relax(): iterate + RELAXATION * (right_side - operate(iterate, conductivity, face_...  2.93 us
    mul x24, other arithmetic, operate(): face_weights[position]  2.55 us
  transfers between devices with their start and end apart: 3, of which 3 were waited for; matrix products, arithmetic and copies ran while one was open for 5% of the time, Pallas kernels for 0%

profile of v1, /device:TPU:0, one launch (start us, length us, event | category | flops | bytes accessed | tf_op | source)
XLA Modules:
  0.0 79.9 jit_solution(9862936214051846149)
XLA Ops:
  7.2 1.0 %exponential_bitcast_fusion = f32[1,1,16,32,128]{4,3,2,1,0:T(8,128)S(1)} fusion(f32[1,16,32,128]{3,2,1,0:T(8,128)} %param.9), kind=kLoop, calls=%fused_computation.45 | loop fusion | bytes 524288 | tf_op jit(solution)/shard_map/vmap()/broadcast_in_dim | solution.py:75
  8.3 0.2 subtract_multiply_fusion
  8.5 0.1 subtract_multiply_fusion.1
  8.6 0.9 %copy-done.2 = f32[1,1,16,32,128]{4,3,2,1,0:T(8,128)S(1)} copy-done((f32[1,1,16,32,128]{4,3,2,1,0:T(8,128)S(1)}, f32[1,1,16,32,128]{4,3,2,1,0:T(8,128)}, u32[]{:S(2)}) %copy-start.2) | copy-done | bytes 262168
  9.5 0.1 subtract_multiply_fusion.2
  9.7 0.7 subtract_multiply_fusion.5
  10.4 0.1 copy.36
  10.5 0.1 pad_bitcast_fusion
  10.6 0.2 fusion.52
  10.8 0.8 %scatter_custom_fusion = f32[65536]{0:T(1024)S(1)} fusion(s32[2]{0:T(128)S(1)} %fusion.52, f32[2]{0:T(128)} %constant.221, f32[]{:T(128)} %constant.82.clone.1), kind=kCustom, calls=%fused_computation.64 | custom fusion | flops 2 | bytes 262656 | tf_op jit(solution)/shard_map/scatter-add | solution.py:69
  11.6 1.4 %divide_add_fusion.6 = (f32[1,1,16,32,128]{4,3,2,1,0:T(8,128)S(1)}, f32[1,1,16,32,128]{4,3,2,1,0:T(8,128)S(1)}) fusion(f32[1,1,16,32,128]{4,3,2,1,0:T(8,128)S(1)} %copy-done.2, f32[1,1,16,32,128]{4,3,2,1,0:T(8,128)S(1)} %bitcast.68, f32[1,1,16,32,127]{4,3,2,1,0:T(8,128)S(1)} %subtract_multiply_fusion.2, ...), kind=kLoop, calls=%fused_computation.41 | loop fusion | flops 1179648 | bytes 2830336 | tf_op jit(solution)/shard_map/vmap()/add | solution.py:58
  13.2 0.1 fusion.10
  13.3 0.3 divide_add_fusion.5
  13.7 0.1 fusion.8
  13.8 0.3 divide_add_fusion.4
  14.2 0.1 fusion.6
  14.3 0.5 copy-done.6
  14.8 0.2 divide_add_fusion.3
  15.1 1.1 %gather_fusion = f32[128]{0:T(128)S(1)} fusion(f32[65536]{0:T(1024)S(1)} %bitcast.72, s32[1024]{0:T(1024)S(1)} %pad_clamp_fusion), kind=kCustom, calls=%fused_computation | custom fusion | bytes 1536 | tf_op jit(solution)/shard_map/vmap()/gather | solution.py:79
  16.3 1.3 %scatter_custom_fusion.1 = f32[65536]{0:T(1024)S(1)} fusion(s32[128]{0:T(128)S(1)} %compare_select_fusion, f32[128]{0:T(128)S(1)} %fusion.55, f32[]{:T(128)} %constant.82.clone.1), kind=kCustom, calls=%fused_computation.62 | custom fusion | flops 128 | bytes 262148 | tf_op jit(solution)/shard_map/vmap()/scatter-add | solution.py:83
  17.6 0.3 divide_add_fusion.2
  18.0 0.1 fusion.4
  18.1 0.3 divide_add_fusion.1
  18.5 0.1 fusion.2
  18.6 0.3 divide_add_fusion
  19.0 0.1 fusion
  19.1 1.0 %bitcast_multiply_fusion = f32[1,16,32,128]{3,2,1,0:T(8,128)} fusion(f32[1,1,16,32,128]{4,3,2,1,0:T(8,128)S(1)} %divide_add_fusion.3, f32[1,1,16,32,128]{4,3,2,1,0:T(8,128)S(1)} %divide_add_fusion, f32[1,1,16,32,128]{4,3,2,1,0:T(8,128)S(1)} %get-tuple-element.12, f32[1,1,16,32,128]{4,3,2,1,0:T(8,128)S(1)} %bitcast.67, f32[1,1,16,32,127]{4,3,2,1,0:T(8,128)S(1)} %fusion, ...), kind=kLoop, calls=%fused_computation.32 | loop fusion | flops 917504 | bytes 2332672 | tf_op jit(solution)/shard_map/vmap()/mul | solution.py:87
  20.1 0.3 convert_add_fusion
  20.4 0.1 copy.27
  20.5 0.7 cholesky.17
  21.2 0.1 copy.28
  21.3 0.1 select_reduce_fusion
  21.4 0.6 compare_reduce_fusion
  22.1 17.7 %all-gather.2.cloned.1.call-done = f32[4,1,65536]{2,1,0:T(1,128)} async-done(((f32[1,1,65536]{2,1,0:T(1,128)}), f32[4,1,65536]{2,1,0:T(1,128)}) %all-gather.2.cloned.1.call-update) | async-done | bytes 1048592 | tf_op jit(solution)/shard_map/all_gather | solution.py:152
  39.7 2.2 %reduce_sum.16 = f32[65536]{0:T(1024)S(1)} reduce(f32[4,1,65536]{2,1,0:T(1,128)} %all-gather.2.cloned.1.call-done, f32[]{:T(128)} %constant.82.clone.1), dimensions={0,1}, to_apply=%region_4.5 | reduce | flops 196608 | bytes 1310724 | tf_op jit(solution)/shard_map/reduce_sum | solution.py:152
  41.9 0.7 dynamic-slice_subtract_fusion
  42.7 5.6 %all-to-all-start = ((f32[1,8,2048]{2,0,1:T(1,128)}), f32[1,8,2048]{2,0,1:T(1,128)S(1)}, u32[]{:S(2)}, u32[]{:S(2)}) async-start(f32[1,8,2048]{2,0,1:T(1,128)} %bitcast.15), calls=%async_computation | async-start | bytes 131072 | tf_op jit(solution)/shard_map/all_to_all | solution.py:158
  48.3 0.6 select_select_fusion
  49.0 0.6 custom-call.10
  49.7 5.5 %all-to-all-done = f32[1,8,2048]{2,0,1:T(1,128)S(1)} async-done(((f32[1,8,2048]{2,0,1:T(1,128)}), f32[1,8,2048]{2,0,1:T(1,128)S(1)}, u32[]{:S(2)}, u32[]{:S(2)}) %all-to-all-start) | async-done | bytes 65568 | tf_op jit(solution)/shard_map/all_to_all | solution.py:158
  55.2 0.3 fusion.27
  55.5 0.2 fusion.39
  55.7 0.7 copy.33
  56.4 3.4 %all-to-all-start.1 = ((f32[8,1,2048]{2,1,0:T(1,128)}), f32[8,1,2048]{2,1,0:T(1,128)S(1)}, u32[]{:S(2)}, u32[]{:S(2)}) async-start(f32[8,1,2048]{2,1,0:T(1,128)} %copy.33), calls=%async_computation.1 | async-start | bytes 131072 | tf_op jit(solution)/shard_map/all_to_all | solution.py:160
  59.7 0.7 fusion.61
  60.4 6.2 %all-to-all-done.1 = f32[8,1,2048]{2,1,0:T(1,128)S(1)} async-done(((f32[8,1,2048]{2,1,0:T(1,128)}), f32[8,1,2048]{2,1,0:T(1,128)S(1)}, u32[]{:S(2)}, u32[]{:S(2)}) %all-to-all-start.1) | async-done | bytes 65568 | tf_op jit(solution)/shard_map/all_to_all | solution.py:160
  66.6 5.8 %all_gather.7 = f32[1,65536]{1,0:T(1,128)S(1)} all-gather(f32[1,16384]{1,0:T(1,128)S(1)} %bitcast.76), channel_id=1, replica_groups=mesh['src'=4,'ep'=8] {'src'}, dimensions={1}, use_global_device_ids=true | all-gather | bytes 327680 | tf_op jit(solution)/shard_map/all_gather | solution.py:161
  72.3 0.7 copy.42
  (39 shorter events, 0.8 us)
Async XLA Ops:
  7.2 1.1 %copy-start.1 = (f32[1,1,16,32,128]{4,3,2,1,0:T(8,128)S(1)}, f32[1,1,16,32,128]{4,3,2,1,0:T(8,128)}, u32[]{:S(2)}) copy-start(f32[1,1,16,32,128]{4,3,2,1,0:T(8,128)} %param.11) | copy-start | bytes 786436
  7.2 32.6 %all-gather.2.cloned.1.call-start = ((), (), s32[]{:S(2)}) async-start(), calls=%async_computation.2 | async-start | bytes 1310720 | tf_op jit(solution)/shard_map/all_gather | solution.py:152
  8.6 1.0 %copy-start.2 = (f32[1,1,16,32,128]{4,3,2,1,0:T(8,128)S(1)}, f32[1,1,16,32,128]{4,3,2,1,0:T(8,128)}, u32[]{:S(2)}) copy-start(f32[1,1,16,32,128]{4,3,2,1,0:T(8,128)} %param.10) | copy-start | bytes 786436
  9.7 0.7 copy-start.5
  10.4 1.2 %copy-start = (f32[1,16,32,128]{3,2,1,0:T(8,128)S(1)}, f32[1,16,32,128]{3,2,1,0:T(8,128)}, u32[]{:S(2)}) copy-start(f32[1,16,32,128]{3,2,1,0:T(8,128)} %param.9) | copy-start | bytes 786436
  14.2 0.7 copy-start.6
  15.1 1.2 %copy-start.7 = (f32[1,1,128]{2,1,0:T(1,128)S(1)}, f32[1,1,128]{2,1,0:T(1,128)}, u32[]{:S(2)}) copy-start(f32[1,1,128]{2,1,0:T(1,128)} %param.14) | copy-start | bytes 1540
  42.7 7.0 %copy-start.3 = (f32[6,2048]{1,0:T(8,128)S(1)}, f32[6,2048]{1,0:T(8,128)}, u32[]{:S(2)}) copy-start(f32[6,2048]{1,0:T(8,128)} %param.16) | copy-start | bytes 147460
  42.7 7.0 %copy-start.4 = (f32[6,2048]{1,0:T(8,128)S(1)}, f32[6,2048]{1,0:T(8,128)}, u32[]{:S(2)}) copy-start(f32[6,2048]{1,0:T(8,128)} %param.15) | copy-start | bytes 147460
  42.7 12.6 %all-to-all-start = ((f32[1,8,2048]{2,0,1:T(1,128)}), f32[1,8,2048]{2,0,1:T(1,128)S(1)}, u32[]{:S(2)}, u32[]{:S(2)}) async-start(f32[1,8,2048]{2,0,1:T(1,128)} %bitcast.15), calls=%async_computation | async-start | bytes 131072 | tf_op jit(solution)/shard_map/all_to_all | solution.py:158
  56.4 10.2 %all-to-all-start.1 = ((f32[8,1,2048]{2,1,0:T(1,128)}), f32[8,1,2048]{2,1,0:T(1,128)S(1)}, u32[]{:S(2)}, u32[]{:S(2)}) async-start(f32[8,1,2048]{2,1,0:T(1,128)} %copy.33), calls=%async_computation.1 | async-start | bytes 131072 | tf_op jit(solution)/shard_map/all_to_all | solution.py:160
Sparse Core Ops, SparseCore 0:
  20.2 19.4 all-gather.1
